TPU v7x, 256 devices: a whole 4x4x8 slice. The times are simulated.
256 devices in a mesh: seq: 32 (over y, z), tensor: 8 (over x, core).
Axes of the slice: x: 4, y: 4, z: 8, core: 2. Of those that a mesh axis runs over, the one named last changes fastest.
Arguments:
- query: bfloat16 [4096, 2048], P('seq', 'tensor')
- suffix_kv: bfloat16 [4096, 4, 2, 128], P('seq'), may hold values from -6 to 6
- segment_ids: int32 [32, 128], P('seq'), may hold values from 0 to 3, never falling along the last dimension, each value on 1 to 64 neighbouring positions
- request_prefix: int32 [32, 4], P('seq'), may hold values from 0 to 3
- prefix_kv: bfloat16 [32768, 4, 2, 128], P('seq')
- shard_prefix: int32 [32], P('seq'), may hold values from 0 to 3, as said below
- residual: bfloat16 [4096, 2048], P('seq'), may hold values from -3.2 to 3.2
- out_weight: bfloat16 [2048, 2048], P('tensor'), may hold values from -0.1875 to 0.1875
- norm_gain: float32 [2048], replicated, may hold values from 0.1 to 1.9
- expert_ids: int32 [4096, 6], P('seq'), may hold values from 0 to 63, all different within a row; in each aligned block of 128 rows (0 to 127, 128 to 255, ...) at most 24 rows name the same one
- gate_weights: float32 [4096, 6], P('seq'), may hold values from 0.05 to 0.5
- expert_in: bfloat16 [64, 2048, 2, 1408], P('seq', None, None, 'tensor'), may hold values from -0.125 to 0.125
- expert_out: bfloat16 [64, 1408, 2048], P('seq', 'tensor'), may hold values from -0.21875 to 0.21875
Outputs:
- attended: bfloat16 [4096, 2048], P('seq', 'tensor')
- layer_out: bfloat16 [4096, 2048], P('seq', 'tensor')
Inputs may be any that keep to these rules, and one draw needn't show every extreme that they name: `segment_ids`: on each seq index the segment numbers never fall along the 128 positions and every number occurs. `shard_prefix`: every prefix owns the same number of shards. `expert_ids`: each row names 6 different experts; within the 128 rows of one seq index no expert is named more than 24 times, and that count is reached.
All inputs are finite; a program needn't handle non-finite values.
Results may differ from a plain program's by a relative error of at most 0.02.
Values may be sent and summed in bfloat16 or wider, within the bound.
No kernel may reach another device: no remote copies, remote signals or barrier semaphores. Data moves between devices by JAX's collectives and lax.ppermute only.
A program may use at most 128 MiB of HBM per device.

v0:
```python
import jax
import jax.numpy as jnp
from jax import lax
from jax.sharding import PartitionSpec as P

QH = 16
KVH = 4


NEG_FLOOR = -1e30


def fold_block(carried, queries, key_rows, values, allowed, score_scale):
    running_max, running_sum, weighted = carried
    scores = (
        jnp.einsum("rhd,kd->rhk", queries, key_rows, preferred_element_type=jnp.float32)
        * score_scale
    )
    scores = jnp.where(allowed[:, None, :], scores, -jnp.inf)
    new_max = jnp.maximum(running_max, jnp.max(scores, axis=2))
    weights = jnp.exp(scores - new_max[:, :, None])
    shrink = jnp.exp(running_max - new_max)
    gathered = jnp.einsum(
        "rhk,kd->rhd", weights.astype(jnp.bfloat16), values, preferred_element_type=jnp.float32
    )
    return (
        new_max,
        running_sum * shrink + jnp.sum(weights, axis=2),
        weighted * shrink[:, :, None] + gathered,
    )


def body(
    query,
    suffix_kv,
    segment_ids,
    request_prefix,
    prefix_kv,
    shard_prefix,
    residual,
    out_weight,
    norm_gain,
    expert_ids,
    gate_weights,
    expert_in,
    expert_out,
):
    tok_rows = query.shape[0]
    head_size = suffix_kv.shape[3]
    heads_here = query.shape[1] // head_size
    kv_head = lax.axis_index("tensor") * heads_here // (QH // KVH)
    score_scale = head_size ** (-0.5)
    queries = query.reshape(tok_rows, heads_here, head_size)
    segments = segment_ids[0]
    requests = jnp.arange(request_prefix.shape[1], dtype=jnp.int32)
    row_prefix = jnp.sum(
        jnp.where(segments[:, None] == requests[None, :], request_prefix[0][None, :], 0), axis=1
    )
    blank_state = (
        jnp.full((tok_rows, heads_here), NEG_FLOOR, jnp.float32),
        jnp.zeros((tok_rows, heads_here), jnp.float32),
        jnp.zeros((tok_rows, heads_here, head_size), jnp.float32),
    )
    shard_len = prefix_kv.shape[0]
    own_cache = lax.dynamic_slice_in_dim(prefix_kv, kv_head, 1, 1).reshape(shard_len, 2 * head_size)
    cache_rows = lax.all_gather(own_cache, "seq", axis=0, tiled=True)
    owners = lax.all_gather(shard_prefix, "seq", axis=0, tiled=True)
    shard_count = owners.shape[0]
    shards = cache_rows.reshape(shard_count, -1, 2, head_size)

    def one_shard(inner_state, shard_item):
        block_rows, shard_owner = shard_item
        matching = row_prefix == shard_owner

        def attend(current):
            allowed = jnp.broadcast_to(matching[:, None], (tok_rows, block_rows.shape[0]))
            return fold_block(
                current, queries, block_rows[:, 0], block_rows[:, 1], allowed, score_scale
            )

        return (lax.cond(jnp.any(matching), attend, lambda current: current, inner_state), None)

    final_state, unused = lax.scan(one_shard, blank_state, (shards, owners))
    carried = final_state
    own_suffix = lax.dynamic_slice_in_dim(suffix_kv, kv_head, 1, 1).reshape(tok_rows, 2, head_size)
    positions = jnp.arange(tok_rows)
    causal = (segments[:, None] == segments[None, :]) & (positions[None, :] <= positions[:, None])
    carried = fold_block(carried, queries, own_suffix[:, 0], own_suffix[:, 1], causal, score_scale)
    running_max, running_sum, weighted = carried
    attention = (
        (weighted / running_sum[:, :, None])
        .reshape(tok_rows, heads_here * head_size)
        .astype(jnp.bfloat16)
    )
    projected = jnp.dot(attention, out_weight, preferred_element_type=jnp.float32)
    model_width = residual.shape[1]
    slice_width = model_width // lax.axis_size("tensor")
    first_col = lax.axis_index("tensor") * slice_width
    shared = lax.psum_scatter(projected, "tensor", scatter_dimension=1, tiled=True)
    hidden_state = (
        lax.dynamic_slice_in_dim(residual, first_col, slice_width, 1).astype(jnp.float32) + shared
    )
    squares = lax.psum(jnp.sum(hidden_state * hidden_state, axis=1), "tensor")
    gain_cols = lax.dynamic_slice_in_dim(norm_gain, first_col, slice_width, 0)
    normed = (
        hidden_state * lax.rsqrt(squares / model_width + 1e-06)[:, None] * gain_cols[None, :]
    ).astype(jnp.bfloat16)
    attended = hidden_state.astype(jnp.bfloat16)
    exp_here = expert_in.shape[0]
    sources = lax.axis_size("seq")
    experts = exp_here * sources
    top_k = expert_ids.shape[1]
    capacity = 2 * tok_rows * top_k // experts
    flat_ids = expert_ids.reshape(-1)
    onehot = (flat_ids[:, None] == jnp.arange(experts, dtype=jnp.int32)[None, :]).astype(jnp.int32)
    slot_index = jnp.sum((jnp.cumsum(onehot, axis=0) - 1) * onehot, axis=1)
    places = flat_ids * capacity + slot_index
    outgoing = (
        jnp.zeros((experts * capacity, slice_width), jnp.bfloat16)
        .at[places]
        .set(jnp.repeat(normed, top_k, axis=0))
    )
    incoming = lax.all_to_all(
        outgoing.reshape(sources, exp_here, capacity, slice_width),
        "seq",
        split_axis=0,
        concat_axis=0,
        tiled=True,
    )
    gate_up = jnp.einsum(
        "sjcd,jdgh->sjcgh",
        lax.all_gather(incoming, "tensor", axis=3, tiled=True),
        expert_in,
        preferred_element_type=jnp.float32,
    )
    hidden = (jax.nn.silu(gate_up[:, :, :, 0]) * gate_up[:, :, :, 1]).astype(jnp.bfloat16)
    group_terms = jnp.einsum(
        "sjch,jhd->sjcd", hidden, expert_out, preferred_element_type=jnp.float32
    )
    expert_rows_out = lax.psum_scatter(
        group_terms.astype(jnp.bfloat16), "tensor", scatter_dimension=3, tiled=True
    )
    returned = lax.all_to_all(expert_rows_out, "seq", split_axis=0, concat_axis=0, tiled=True)
    picked = returned.reshape(experts * capacity, slice_width)[places].reshape(
        tok_rows, top_k, slice_width
    )
    mixture = jnp.sum(gate_weights[:, :, None] * picked.astype(jnp.float32), axis=1)
    layer_out = (hidden_state + mixture).astype(jnp.bfloat16)
    return (attended, layer_out)


def solution(mesh):
    in_specs = (
        P("seq", "tensor"),
        P("seq", None, None, None),
        P("seq", None),
        P("seq", None),
        P("seq", None, None, None),
        P("seq"),
        P("seq", None),
        P("tensor", None),
        P(),
        P("seq", None),
        P("seq", None),
        P("seq", None, None, "tensor"),
        P("seq", "tensor", None),
    )
    out_specs = (P("seq", "tensor"), P("seq", "tensor"))
    return jax.shard_map(body, mesh=mesh, in_specs=in_specs, out_specs=out_specs, check_vma=False)
```

profile of v0, /device:TPU:32, one launch (start us, length us, event | category | flops | bytes accessed | tf_op | source)
XLA Modules:
  0.0 573.8 jit_solution(9225628321920478958)
XLA Ops:
  7.3 1.6 constant_dynamic-slice_fusion.1
  14.0 23.0 %all-reduce = s32[32]{0:T(128)S(1)} all-reduce(s32[32]{0:T(128)S(1)} %dynamic-update-slice), channel_id=1, replica_groups=mesh['seq'=32,'tensor'=8] {'seq'}, use_global_device_ids=true, to_apply=%add | all-reduce | flops 32 | bytes 256
  37.4 113.8 %all-gather.3.cloned.1.call-done = bf16[32768,256]{0,1:T(8,128)(2,1)} async-done(((bf16[1024,256]{0,1:T(8,128)(2,1)}), bf16[32768,256]{0,1:T(8,128)(2,1)}) %all-gather.3.cloned.1.call-update) | async-done | bytes 16777232 | tf_op jit(solution)/shard_map/all_gather | solution.py:66
  151.2 18.7 %copy.104 = bf16[32,8,32,1024]{3,2,1,0:T(8,128)(2,1)} copy(bf16[32,8,32,1024]{3,1,2,0:T(8,128)(2,1)} %bitcast.106) | data formatting | bytes 33554432
  169.8 23.0 %copy.78 = bf16[32,1024,2,128]{3,1,2,0:T(8,128)(2,1)} copy(bf16[32,1024,2,128]{1,0,3,2:T(8,128)(2,1)} %bitcast.105) | data formatting | bytes 33554432 | tf_op jit(solution)/shard_map/while | solution.py:83
  192.9 95.2 %while.14 = (s32[]{:T(128)}, f32[128,2]{0,1:T(2,128)S(1)}, f32[128,2]{0,1:T(2,128)S(1)}, f32[128,2,128]{2,0,1:T(8,128)S(1)}, s32[32]{0:T(128)S(1)}, /*index=5*/s...) while((s32[]{:T(128)}, f32[128,2]{0,1:T(2,128)S(1)}, ...), condition=%wide.region_7.8_spmd, body=%wide.region_1.7_spmd.sunk | while | flops 136119040 | bytes 5064039 | solution.py:83
  195.9 1.3 fusion.45
  205.8 1.3 fusion.45
  207.6 2.0 conditional.2
  214.6 2.1 conditional.2
  221.6 2.1 conditional.2
  228.6 2.0 conditional.2
  233.1 2.1 conditional.2
  249.9 2.0 conditional.2
  256.8 2.1 conditional.2
  286.0 2.0 conditional.2
  288.5 2.6 fusion.39
  291.6 1.8 reduce-window.6
  294.9 76.3 %reduce-scatter.3.cloned.1.call-done = f32[128,256]{1,0:T(8,128)} async-done(((f32[128,2048]{1,0:T(8,128)}), f32[128,256]{1,0:T(8,128)}) %reduce-scatter.3.cloned.1.call-update) | async-done | bytes 131088 | tf_op jit(solution)/shard_map/reduce_scatter | solution.py:99
  372.2 12.9 %psum.7 = f32[128]{0:T(128)S(1)} all-reduce(f32[128]{0:T(128)S(1)} %multiply_reduce_fusion.1), channel_id=1, replica_groups=mesh['seq'=32,'tensor'=8] {'tensor'}, use_global_device_ids=true, to_apply=%region_15.16 | all-reduce | flops 128 | bytes 1024 | tf_op jit(solution)/shard_map/psum | solution.py:103
  387.0 6.7 %scatter_custom_fusion = bf16[1536,256]{1,0:T(8,128)(2,1)} fusion(s32[768]{0:T(1024)S(1)} %fusion.33, bf16[768,256]{1,0:T(8,128)(2,1)} %reshape.146, bf16[]{:T(256)} %constant.72.clone.1), kind=kCustom, calls=%fused_computation.34 | custom fusion | bytes 786944 | tf_op jit(solution)/shard_map/scatter | solution.py:121
  393.8 32.8 %all_to_all.10 = bf16[32,2,24,256]{3,2,1,0:T(8,128)(2,1)S(1)} all-to-all(bf16[32,2,24,256]{3,2,1,0:T(8,128)(2,1)} %bitcast.107), channel_id=1, replica_groups=mesh['seq'=32,'tensor'=8] {'seq'}, dimensions={0} | all-to-all | bytes 1572864 | tf_op jit(solution)/shard_map/all_to_all | solution.py:123
  427.7 40.6 %all-gather.5.cloned.1.call-done = bf16[32,2,24,2048]{3,2,0,1:T(8,128)(2,1)} async-done(((bf16[32,2,24,256]{3,2,0,1:T(8,128)(2,1)}), bf16[32,2,24,2048]{3,2,0,1:T(8,128)(2,1)}) %all-gather.5.cloned.1.call-update) | async-done | bytes 6291472 | tf_op jit(solution)/shard_map/all_gather | solution.py:132
  468.3 5.7 fusion.9
  474.0 4.6 convert_bitcast_fusion
  478.6 46.1 %reduce-scatter.5.cloned.1.call-done = bf16[32,2,24,256]{3,2,0,1:T(8,128)(2,1)} async-done(((bf16[32,2,24,2048]{3,2,0,1:T(8,128)(2,1)}), bf16[32,2,24,256]{3,2,0,1:T(8,128)(2,1)}) %reduce-scatter.5.cloned.1.call-update) | async-done | bytes 786448 | tf_op jit(solution)/shard_map/reduce_scatter | solution.py:140
  524.8 2.1 copy.92
  526.8 10.1 %all-to-all-start.1 = ((bf16[32,2,24,256]{3,2,1,0:T(8,128)(2,1)}), bf16[32,2,24,256]{3,2,1,0:T(8,128)(2,1)}, u32[]{:S(2)}, u32[]{:S(2)}) async-start(bf16[32,2,24,256]{3,2,1,0:T(8,128)(2,1)} %copy.92), calls=%async_computation.3 | async-start | bytes 1572864 | tf_op jit(solution)/shard_map/all_to_all | solution.py:143
  537.1 22.6 %all-to-all-done.1 = bf16[32,2,24,256]{3,2,1,0:T(8,128)(2,1)} async-done(((bf16[32,2,24,256]{3,2,1,0:T(8,128)(2,1)}), bf16[32,2,24,256]{3,2,1,0:T(8,128)(2,1)}, u32[]{:S(2)}, u32[]{:S(2)}) %all-to-all-start.1) | async-done | bytes 786464 | tf_op jit(solution)/shard_map/all_to_all | solution.py:143
  559.7 3.4 gather_fusion
  564.1 1.6 multiply_reduce_fusion
  565.7 1.5 add_convert_fusion
  (206 shorter events, 85.9 us)
Async XLA Ops:
  7.2 461.2 %copy-start = (bf16[2,2048,2,176]{1,3,2,0:T(8,128)(2,1)S(1)}, bf16[2,2048,2,176]{1,3,2,0:T(8,128)(2,1)}, u32[]{:S(2)}) copy-start(bf16[2,2048,2,176]{1,3,2,0:T(8,128)(2,1)} %param.28) | copy-start | bytes 8650756
  7.2 5.5 copy-start.7
  7.2 29.8 %copy-start.4 = (s32[1,128]{1,0:T(1,128)S(1)}, s32[1,128]{1,0:T(1,128)}, u32[]{:S(2)}) copy-start(s32[1,128]{1,0:T(1,128)} %param.19) | copy-start | bytes 1540
  7.2 29.8 %copy-start.6 = (s32[1,4]{1,0:T(1,128)S(1)}, s32[1,4]{1,0:T(1,128)}, u32[]{:S(2)}) copy-start(s32[1,4]{1,0:T(1,128)} %param.20) | copy-start | bytes 52
  7.2 144.0 %all-gather.3.cloned.1.call-start = ((), (), s32[]{:S(2)}) async-start(), calls=%async_computation.4 | async-start | bytes 17301504 | tf_op jit(solution)/shard_map/all_gather | solution.py:66
  10.0 361.2 %reduce-scatter.3.cloned.1.call-start = ((), (), s32[]{:S(2)}) async-start(), calls=%async_computation.5 | async-start | bytes 1179648 | tf_op jit(solution)/shard_map/reduce_scatter | solution.py:99
  288.1 3.0 copy-start.2
  291.1 177.2 %all-gather.5.cloned.1.call-start = ((), (), s32[]{:S(2)}) async-start(), calls=%async_computation.6 | async-start | bytes 7077888 | tf_op jit(solution)/shard_map/all_gather | solution.py:132
  427.5 97.3 %reduce-scatter.5.cloned.1.call-start = ((), (), s32[]{:S(2)}) async-start(), calls=%async_computation.7 | async-start | bytes 7077888 | tf_op jit(solution)/shard_map/reduce_scatter | solution.py:140
  468.3 5.7 copy-start.5
  478.6 58.4 %copy-start.3 = (f32[128,6]{0,1:T(8,128)S(1)}, f32[128,6]{0,1:T(8,128)}, u32[]{:S(2)}) copy-start(f32[128,6]{0,1:T(8,128)} %param.27) | copy-start | bytes 9220
  526.8 32.8 %all-to-all-start.1 = ((bf16[32,2,24,256]{3,2,1,0:T(8,128)(2,1)}), bf16[32,2,24,256]{3,2,1,0:T(8,128)(2,1)}, u32[]{:S(2)}, u32[]{:S(2)}) async-start(bf16[32,2,24,256]{3,2,1,0:T(8,128)(2,1)} %copy.92), calls=%async_computation.3 | async-start | bytes 1572864 | tf_op jit(solution)/shard_map/all_to_all | solution.py:143
  559.7 6.1 %copy-start.1 = (f32[128,256]{1,0:T(8,128)S(1)}, f32[128,256]{1,0:T(8,128)}, u32[]{:S(2)}) copy-start(f32[128,256]{1,0:T(8,128)} %reduce-scatter.3.cloned.1.call-done) | copy-start | bytes 393220
Sparse Core Ops, SparseCore 0:
  10.6 140.5 all-gather.2
  291.2 79.9 reduce-scatter.2
  427.6 40.6 all-gather.4
  478.7 45.9 reduce-scatter.4
where the time goes:
time: 577 us; the launch traced here: 574 us
  waiting for transfers between devices  299 us (52%)
  local copies, waits for them, and re-layouts  92.2 us (16%)
  blocking collectives  68.7 us (12%)
  other arithmetic  49.5 us (9%)
  loops' own time  19.7 us (3%)
  matrix products  19.1 us (3%)
  between operations  14.7 us (3%)
  starting transfers between devices  10.5 us (2%)
    all_gather x1, waiting for transfers between devices, body(): cache_rows = lax.all_gather(own_cache, 'seq', axis=0, tiled=True)  114 us
    reduce_scatter x1, waiting for transfers between devices, body(): lax.psum_scatter(projected, 'tensor', scatter_dimension=1, tiled=True)  76.3 us
    reduce_scatter x1, waiting for transfers between devices, body(): lax.psum_scatter(group_terms.astype(jnp.bfloat16), 'tensor', scatter_dime...  46.1 us
    reduce_or x32, other arithmetic, one_shard(): jnp.any(matching)  40.7 us
    all_gather x1, waiting for transfers between devices, body(): lax.all_gather(incoming, 'tensor', axis=3, tiled=True)  40.6 us
    all_to_all x1, blocking collectives, body(): lax.all_to_all(outgoing.reshape(sources, exp_here, capacity, slice_width)...  32.8 us
    while x3, local copies, waits for them, and re-layouts, body(): final_state, unused = lax.scan(one_shard, blank_state, (shards, owners))  23.2 us
    unnamed x1, blocking collectives  23 us
  transfers between devices with their start and end apart: 5, of which 5 were waited for; matrix products, arithmetic and copies ran while one was open for 1% of the time, Pallas kernels for 0%

commit v1 on v0

--- a/solution.py
+++ b/solution.py
@@ -1,6 +1,10 @@
+import functools
+
 import jax
 import jax.numpy as jnp
 from jax import lax
+from jax.experimental import pallas as pl
+from jax.experimental.pallas import tpu as pltpu
 from jax.sharding import PartitionSpec as P
 
 QH = 16
@@ -8,26 +12,64 @@
 
 
 NEG_FLOOR = -1e30
-
-
-def fold_block(carried, queries, key_rows, values, allowed, score_scale):
-    running_max, running_sum, weighted = carried
+NEG_SHIFT = -(2.0 ** 100)
+TOKEN_BLOCKS = 4
+
+
+def split3(x):
+    hi = x.astype(jnp.bfloat16).astype(jnp.float32)
+    rest = x - hi
+    mid = rest.astype(jnp.bfloat16).astype(jnp.float32)
+    lo = (rest - mid).astype(jnp.bfloat16).astype(jnp.float32)
+    return hi, mid, lo
+
+
+def shard_kernel(q_ref, k_ref, v_ref, o_ref, st_ref, *, score_scale):
+    blocks, rows, width = q_ref.shape
+    q = q_ref[...].reshape(blocks * rows, width)
     scores = (
-        jnp.einsum("rhd,kd->rhk", queries, key_rows, preferred_element_type=jnp.float32)
+        lax.dot_general(
+            q, k_ref[...], (((1,), (1,)), ((), ())), preferred_element_type=jnp.float32
+        )
         * score_scale
     )
-    scores = jnp.where(allowed[:, None, :], scores, -jnp.inf)
-    new_max = jnp.maximum(running_max, jnp.max(scores, axis=2))
-    weights = jnp.exp(scores - new_max[:, :, None])
-    shrink = jnp.exp(running_max - new_max)
-    gathered = jnp.einsum(
-        "rhk,kd->rhd", weights.astype(jnp.bfloat16), values, preferred_element_type=jnp.float32
-    )
-    return (
-        new_max,
-        running_sum * shrink + jnp.sum(weights, axis=2),
-        weighted * shrink[:, :, None] + gathered,
-    )
+    shift = jnp.max(scores, axis=1, keepdims=True)
+    weights = jnp.exp(scores - shift)
+    total = jnp.sum(weights, axis=1, keepdims=True)
+    gathered = jnp.dot(
+        weights.astype(jnp.bfloat16), v_ref[...], preferred_element_type=jnp.float32
+    )
+    o_ref[...] = gathered.astype(jnp.bfloat16).reshape(blocks, 1, rows, width)
+    parts = split3(shift) + split3(total)
+    for col, part in enumerate(parts):
+        st_ref[0, :, col : col + 1] = part
+    st_ref[0, :, 6:8] = jnp.zeros((blocks * rows, 2), jnp.float32)
+
+
+def shard_attention(gathered_q, keys, values, score_scale):
+    sources, padded_rows, two_heads = gathered_q.shape
+    head_size = keys.shape[1]
+    rows = padded_rows - 1
+    heads = two_heads // head_size
+    tb = TOKEN_BLOCKS
+    kernel = functools.partial(shard_kernel, score_scale=score_scale)
+    return pl.pallas_call(
+        kernel,
+        grid=(sources // tb, heads),
+        in_specs=[
+            pl.BlockSpec((tb, rows, head_size), lambda b, h: (b, 0, h)),
+            pl.BlockSpec(keys.shape, lambda b, h: (0, 0)),
+            pl.BlockSpec(values.shape, lambda b, h: (0, 0)),
+        ],
+        out_specs=[
+            pl.BlockSpec((tb, 1, rows, head_size), lambda b, h: (b, h, 0, 0)),
+            pl.BlockSpec((1, tb * rows, 8), lambda b, h: (h, b, 0)),
+        ],
+        out_shape=[
+            jax.ShapeDtypeStruct((sources, heads, rows, head_size), jnp.bfloat16),
+            jax.ShapeDtypeStruct((heads, sources * rows, 8), jnp.float32),
+        ],
+    )(gathered_q, keys, values)
 
 
 def body(
@@ -56,39 +98,52 @@
     row_prefix = jnp.sum(
         jnp.where(segments[:, None] == requests[None, :], request_prefix[0][None, :], 0), axis=1
     )
-    blank_state = (
-        jnp.full((tok_rows, heads_here), NEG_FLOOR, jnp.float32),
-        jnp.zeros((tok_rows, heads_here), jnp.float32),
-        jnp.zeros((tok_rows, heads_here, head_size), jnp.float32),
-    )
-    shard_len = prefix_kv.shape[0]
-    own_cache = lax.dynamic_slice_in_dim(prefix_kv, kv_head, 1, 1).reshape(shard_len, 2 * head_size)
-    cache_rows = lax.all_gather(own_cache, "seq", axis=0, tiled=True)
-    owners = lax.all_gather(shard_prefix, "seq", axis=0, tiled=True)
-    shard_count = owners.shape[0]
-    shards = cache_rows.reshape(shard_count, -1, 2, head_size)
-
-    def one_shard(inner_state, shard_item):
-        block_rows, shard_owner = shard_item
-        matching = row_prefix == shard_owner
-
-        def attend(current):
-            allowed = jnp.broadcast_to(matching[:, None], (tok_rows, block_rows.shape[0]))
-            return fold_block(
-                current, queries, block_rows[:, 0], block_rows[:, 1], allowed, score_scale
-            )
-
-        return (lax.cond(jnp.any(matching), attend, lambda current: current, inner_state), None)
-
-    final_state, unused = lax.scan(one_shard, blank_state, (shards, owners))
-    carried = final_state
+    prefix_row = jnp.zeros((1, query.shape[1]), jnp.bfloat16).at[0, :tok_rows].set(
+        row_prefix.astype(jnp.bfloat16)
+    )
+    gathered_q = lax.all_gather(
+        jnp.concatenate([query, prefix_row], axis=0), "seq", axis=0, tiled=False
+    )
+    sources = gathered_q.shape[0]
+    own_cache = lax.dynamic_slice_in_dim(prefix_kv, kv_head, 1, 1)[:, 0]
+    part_o, part_st = shard_attention(
+        gathered_q, own_cache[:, 0], own_cache[:, 1], score_scale
+    )
+    valid = gathered_q[:, tok_rows, :tok_rows] == shard_prefix[0].astype(jnp.bfloat16)
+    stats = part_st.reshape(heads_here, sources, tok_rows, 8)
+    keep = valid[None, :, :, None]
+    column = jnp.arange(8)[None, None, None, :]
+    stats = jnp.where(keep, stats, jnp.where(column == 0, NEG_SHIFT, 0.0))
+    stats = jnp.transpose(stats, (1, 0, 3, 2)).astype(jnp.bfloat16)
+    outgoing = jnp.concatenate([part_o, stats], axis=2)
+    returned = lax.all_to_all(outgoing, "seq", split_axis=0, concat_axis=0, tiled=True)
+    got_o = returned[:, :, :tok_rows, :].astype(jnp.float32)
+    got_st = returned[:, :, tok_rows:, :].astype(jnp.float32)
+    got_shift = got_st[:, :, 0] + got_st[:, :, 1] + got_st[:, :, 2]
+    got_total = got_st[:, :, 3] + got_st[:, :, 4] + got_st[:, :, 5]
+
     own_suffix = lax.dynamic_slice_in_dim(suffix_kv, kv_head, 1, 1).reshape(tok_rows, 2, head_size)
     positions = jnp.arange(tok_rows)
     causal = (segments[:, None] == segments[None, :]) & (positions[None, :] <= positions[:, None])
-    carried = fold_block(carried, queries, own_suffix[:, 0], own_suffix[:, 1], causal, score_scale)
-    running_max, running_sum, weighted = carried
+    suf_scores = (
+        jnp.einsum("rhd,kd->hrk", queries, own_suffix[:, 0], preferred_element_type=jnp.float32)
+        * score_scale
+    )
+    suf_scores = jnp.where(causal[None], suf_scores, -jnp.inf)
+    suf_shift = jnp.max(suf_scores, axis=2)
+    suf_weights = jnp.exp(suf_scores - suf_shift[:, :, None])
+    suf_total = jnp.sum(suf_weights, axis=2)
+    suf_o = jnp.einsum(
+        "hrk,kd->hrd", suf_weights.astype(jnp.bfloat16), own_suffix[:, 1],
+        preferred_element_type=jnp.float32,
+    )
+    common = jnp.maximum(suf_shift, jnp.max(got_shift, axis=0))
+    got_scale = jnp.exp(got_shift - common[None])
+    suf_scale = jnp.exp(suf_shift - common)
+    numer = jnp.sum(got_o * got_scale[..., None], axis=0) + suf_o * suf_scale[..., None]
+    denom = jnp.sum(got_total * got_scale, axis=0) + suf_total * suf_scale
     attention = (
-        (weighted / running_sum[:, :, None])
+        jnp.transpose(numer / denom[..., None], (1, 0, 2))
         .reshape(tok_rows, heads_here * head_size)
         .astype(jnp.bfloat16)
     )

time: 577 us -> 425 us (0.74)
  local copies, waits for them, and re-layouts: 92.2 us -> 23.7 us
  waiting for transfers between devices: 299 us -> 261 us
  other arithmetic: 49.5 us -> 18.5 us
  Pallas kernels: 0 us -> 29.1 us
  blocking collectives: 68.7 us -> 45.8 us
  loops' own time: 19.7 us -> 0 us
  starting transfers between devices: 10.5 us -> 17.7 us
  matrix products: 19.1 us -> 13.2 us
    reduce_scatter x1, waiting for transfers between devices: 76.3 us -> 28.3 us  [body(): lax.psum_scatter(projected, 'tensor', scatter_dimension=1, tiled=True)]
    all_to_all x0 -> x1, waiting for transfers between devices: none -> 46.9 us  [body(): lax.all_to_all(outgoing, 'seq', split_axis=0, concat_axis=0, tiled=True)]
    reduce_or x32 -> x0, other arithmetic: 40.7 us -> none  [one_shard(): jnp.any(matching)]
    all_gather x1, waiting for transfers between devices: 114 us -> 76.8 us  [body(): lax.all_gather(jnp.concatenate([query, prefix_row], axis=0), 'seq', axis=...]
    pallas_call x0 -> x1, Pallas kernels: none -> 29.1 us  [shard_attention(): pl.pallas_call(kernel, grid=(sources // tb, heads), in_specs=[pl.BlockSpe...]
    while x3 -> x0, local copies, waits for them, and re-layouts: 23.2 us -> none  [body(): final_state, unused = lax.scan(one_shard, blank_state, (shards, owners))]
    unnamed x1 -> x0, blocking collectives: 23 us -> none
    unnamed x24 -> x16, local copies, waits for them, and re-layouts: 22.3 us -> 0.26 us
  transfers between devices with their start and end apart: 5 -> 6, of which waited for: 5 -> 6; matrix products, arithmetic and copies ran while one was open for 1% -> 2% of each run, Pallas kernels for 0% -> 0%
where the time goes in v1:
time: 425 us; the launch traced here: 424 us
  waiting for transfers between devices  261 us (61%)
  blocking collectives  45.8 us (11%)
  Pallas kernels  29.1 us (7%)
  local copies, waits for them, and re-layouts  23.7 us (6%)
  other arithmetic  18.5 us (4%)
  starting transfers between devices  17.7 us (4%)
  between operations  14.8 us (3%)
  matrix products  13.2 us (3%)
    all_gather x1, waiting for transfers between devices, body(): lax.all_gather(jnp.concatenate([query, prefix_row], axis=0), 'seq', axis=...  76.8 us
    all_to_all x1, waiting for transfers between devices, body(): lax.all_to_all(outgoing, 'seq', split_axis=0, concat_axis=0, tiled=True)  46.9 us
    reduce_scatter x1, waiting for transfers between devices, body(): lax.psum_scatter(group_terms.astype(jnp.bfloat16), 'tensor', scatter_dime...  46.1 us
    all_gather x1, waiting for transfers between devices, body(): lax.all_gather(incoming, 'tensor', axis=3, tiled=True)  40.6 us
    all_to_all x1, blocking collectives, body(): lax.all_to_all(outgoing.reshape(sources, exp_here, capacity, slice_width)...  32.9 us
    pallas_call x1, Pallas kernels, shard_attention(): pl.pallas_call(kernel, grid=(sources // tb, heads), in_specs=[pl.BlockSpe...  29.1 us
    reduce_scatter x1, waiting for transfers between devices, body(): lax.psum_scatter(projected, 'tensor', scatter_dimension=1, tiled=True)  28.3 us
    all_to_all x1, waiting for transfers between devices, body(): lax.all_to_all(expert_rows_out, 'seq', split_axis=0, concat_axis=0, tiled...  22.6 us
  transfers between devices with their start and end apart: 6, of which 6 were waited for; matrix products, arithmetic and copies ran while one was open for 2% of the time, Pallas kernels for 0%

profile of v1, /device:TPU:32, one launch (start us, length us, event | category | flops | bytes accessed | tf_op | source)
XLA Modules:
  0.0 424.1 jit_solution(11754211464005246081)
XLA Ops:
  7.9 0.9 select_reduce_fusion
  9.4 1.5 fusion.29
  11.0 1.4 constant_dynamic-slice_fusion.1
  14.0 76.8 %all-gather.7.cloned.1.call-done.q_ref = bf16[32,129,256]{2,1,0:T(8,128)(2,1)} async-done(((bf16[1,129,256]{2,1,0:T(8,128)(2,1)}), bf16[32,129,256]{2,1,0:T(8,128)(2,1)}) %all-gather.7.cloned.1.call-update) | async-done | bytes 2113552 | tf_op jit(solution)/shard_map/all_gather | solution.py:104
  90.8 29.1 %shard_map.140 = (bf16[32,2,128,128]{3,2,1,0:T(8,128)(2,1)}, f32[2,4096,8]{2,1,0:T(8,128)}) custom-call(bf16[32,129,256]{2,1,0:T(8,128)(2,1)} %all-gather.7.cloned.1.call-done.q_ref, bf16[1024,128]{1,0:T(8,128)(2,1)} %get-tuple-element.25.k_ref, bf16[1024,128]{1,0:T(8,128)(2,1)} %get-tuple-element.24.v_ref), custom_call_target="tpu_custom_call" | custom-call | tf_op jit(solution)/shard_map/pallas_call | solution.py:56
  119.9 2.5 copy.64
  123.4 3.2 pad_maximum_fusion
  126.6 7.2 %all-to-all-start = ((bf16[32,2,136,128]{3,2,1,0:T(8,128)(2,1)}), bf16[32,2,136,128]{3,2,1,0:T(8,128)(2,1)}, u32[]{:S(2)}, u32[]{:S(2)}) async-start(bf16[32,2,136,128]{3,2,1,0:T(8,128)(2,1)} %pad_maximum_fusion), calls=%async_computation | async-start | bytes 4456448 | tf_op jit(solution)/shard_map/all_to_all | solution.py:119
  133.8 0.9 constant_dynamic-slice_fusion
  135.1 46.9 %all-to-all-done = bf16[32,2,136,128]{3,2,1,0:T(8,128)(2,1)} async-done(((bf16[32,2,136,128]{3,2,1,0:T(8,128)(2,1)}), bf16[32,2,136,128]{3,2,1,0:T(8,128)(2,1)}, u32[]{:S(2)}, u32[]{:S(2)}) %all-to-all-start) | async-done | bytes 2228256 | tf_op jit(solution)/shard_map/all_to_all | solution.py:119
  182.1 0.9 slice_convert_fusion
  183.2 3.1 multiply_reduce_fusion
  186.7 2.6 fusion.47
  189.8 1.8 reduce-window.6
  193.1 28.3 %reduce-scatter.3.cloned.1.call-done = f32[128,256]{1,0:T(8,128)} async-done(((f32[128,2048]{1,0:T(8,128)}), f32[128,256]{1,0:T(8,128)}) %reduce-scatter.3.cloned.1.call-update) | async-done | bytes 131088 | tf_op jit(solution)/shard_map/reduce_scatter | solution.py:154
  221.4 1.0 multiply_reduce_fusion.2
  222.4 12.9 %psum.7 = f32[128]{0:T(128)S(1)} all-reduce(f32[128]{0:T(128)S(1)} %multiply_reduce_fusion.2), channel_id=1, replica_groups=mesh['seq'=32,'tensor'=8] {'tensor'}, use_global_device_ids=true, to_apply=%region_12.13 | all-reduce | flops 128 | bytes 1024 | tf_op jit(solution)/shard_map/psum | solution.py:158
  235.3 1.0 multiply_convert_fusion
  237.3 6.7 %scatter_custom_fusion = bf16[1536,256]{1,0:T(8,128)(2,1)} fusion(s32[768]{0:T(1024)S(1)} %fusion.36, bf16[768,256]{1,0:T(8,128)(2,1)} %reshape.241, bf16[]{:T(256)} %constant.71.clone.1), kind=kCustom, calls=%fused_computation.25 | custom fusion | bytes 786944 | tf_op jit(solution)/shard_map/scatter | solution.py:176
  244.0 32.9 %all_to_all.15 = bf16[32,2,24,256]{3,2,1,0:T(8,128)(2,1)S(1)} all-to-all(bf16[32,2,24,256]{3,2,1,0:T(8,128)(2,1)} %bitcast.138), channel_id=1, replica_groups=mesh['seq'=32,'tensor'=8] {'seq'}, dimensions={0} | all-to-all | bytes 1572864 | tf_op jit(solution)/shard_map/all_to_all | solution.py:178
  276.9 0.9 copy.78
  278.0 40.6 %all-gather.5.cloned.1.call-done = bf16[32,2,24,2048]{3,2,0,1:T(8,128)(2,1)} async-done(((bf16[32,2,24,256]{3,2,0,1:T(8,128)(2,1)}), bf16[32,2,24,2048]{3,2,0,1:T(8,128)(2,1)}) %all-gather.5.cloned.1.call-update) | async-done | bytes 6291472 | tf_op jit(solution)/shard_map/all_gather | solution.py:187
  318.6 5.7 %fusion.3 = f32[32,2,24,2,176]{4,2,3,0,1:T(8,128)S(1)} fusion(bf16[2,2048,2,176]{1,3,2,0:T(8,128)(2,1)S(1)} %copy-done, bf16[32,2,24,2048]{3,2,0,1:T(8,128)(2,1)} %all-gather.5.cloned.1.call-done), kind=kOutput, calls=%fused_computation.8 | convolution fusion | flops 2214592512 | bytes 11337728 | tf_op jit(solution)/shard_map/sjcd,jdgh->sjcgh/dot_general | solution.py:185
  324.3 4.6 %convert_bitcast_fusion = bf16[32,2,24,2048]{3,2,0,1:T(8,128)(2,1)} fusion(bf16[2,176,2048]{2,1,0:T(8,128)(2,1)S(1)} %copy-done.6, f32[32,2,24,2,176]{4,2,3,0,1:T(8,128)S(1)} %fusion.3), kind=kOutput, calls=%fused_computation.4 | convolution fusion | flops 1112064000 | bytes 9895936 | tf_op jit(solution)/shard_map/sjch,jhd->sjcd/dot_general | solution.py:192
  328.9 46.1 %reduce-scatter.5.cloned.1.call-done = bf16[32,2,24,256]{3,2,0,1:T(8,128)(2,1)} async-done(((bf16[32,2,24,2048]{3,2,0,1:T(8,128)(2,1)}), bf16[32,2,24,256]{3,2,0,1:T(8,128)(2,1)}) %reduce-scatter.5.cloned.1.call-update) | async-done | bytes 786448 | tf_op jit(solution)/shard_map/reduce_scatter | solution.py:195
  375.0 2.1 copy.80
  377.1 10.1 %all-to-all-start.2 = ((bf16[32,2,24,256]{3,2,1,0:T(8,128)(2,1)}), bf16[32,2,24,256]{3,2,1,0:T(8,128)(2,1)}, u32[]{:S(2)}, u32[]{:S(2)}) async-start(bf16[32,2,24,256]{3,2,1,0:T(8,128)(2,1)} %copy.80), calls=%async_computation.4 | async-start | bytes 1572864 | tf_op jit(solution)/shard_map/all_to_all | solution.py:198
  387.4 22.6 %all-to-all-done.2 = bf16[32,2,24,256]{3,2,1,0:T(8,128)(2,1)} async-done(((bf16[32,2,24,256]{3,2,1,0:T(8,128)(2,1)}), bf16[32,2,24,256]{3,2,1,0:T(8,128)(2,1)}, u32[]{:S(2)}, u32[]{:S(2)}) %all-to-all-start.2) | async-done | bytes 786464 | tf_op jit(solution)/shard_map/all_to_all | solution.py:198
  410.0 3.3 gather_fusion
  413.3 1.1 reshape.228
  414.4 1.6 multiply_reduce_fusion.1
  416.0 1.5 add_convert_fusion
  (58 shorter events, 7.5 us)
Async XLA Ops:
  7.2 311.5 %copy-start = (bf16[2,2048,2,176]{1,3,2,0:T(8,128)(2,1)S(1)}, bf16[2,2048,2,176]{1,3,2,0:T(8,128)(2,1)}, u32[]{:S(2)}) copy-start(bf16[2,2048,2,176]{1,3,2,0:T(8,128)(2,1)} %param.26) | copy-start | bytes 8650756
  7.2 83.6 %all-gather.7.cloned.1.call-start = ((), (), s32[]{:S(2)}) async-start(), calls=%async_computation.8 | async-start | bytes 2297856 | tf_op jit(solution)/shard_map/all_gather | solution.py:104
  126.6 8.2 %copy-start.5 = (s32[1,128]{1,0:T(1,128)S(1)}, s32[1,128]{1,0:T(1,128)}, u32[]{:S(2)}) copy-start(s32[1,128]{1,0:T(1,128)} %param.17) | copy-start | bytes 1540
  126.6 8.3 %copy-start.2 = (bf16[128,256]{1,0:T(8,128)(2,1)S(1)}, bf16[128,256]{1,0:T(8,128)(2,1)}, u32[]{:S(2)}) copy-start(bf16[128,256]{1,0:T(8,128)(2,1)} %param.15) | copy-start | bytes 196612
  126.6 55.5 %all-to-all-start = ((bf16[32,2,136,128]{3,2,1,0:T(8,128)(2,1)}), bf16[32,2,136,128]{3,2,1,0:T(8,128)(2,1)}, u32[]{:S(2)}, u32[]{:S(2)}) async-start(bf16[32,2,136,128]{3,2,1,0:T(8,128)(2,1)} %pad_maximum_fusion), calls=%async_computation | async-start | bytes 4456448 | tf_op jit(solution)/shard_map/all_to_all | solution.py:119
  133.8 87.6 %reduce-scatter.3.cloned.1.call-start = ((), (), s32[]{:S(2)}) async-start(), calls=%async_computation.5 | async-start | bytes 1179648 | tf_op jit(solution)/shard_map/reduce_scatter | solution.py:154
  186.4 3.0 copy-start.3
  189.3 129.3 %all-gather.5.cloned.1.call-start = ((), (), s32[]{:S(2)}) async-start(), calls=%async_computation.6 | async-start | bytes 7077888 | tf_op jit(solution)/shard_map/all_gather | solution.py:187
  277.8 97.2 %reduce-scatter.5.cloned.1.call-start = ((), (), s32[]{:S(2)}) async-start(), calls=%async_computation.7 | async-start | bytes 7077888 | tf_op jit(solution)/shard_map/reduce_scatter | solution.py:195
  318.6 5.7 %copy-start.6 = (bf16[2,176,2048]{2,1,0:T(8,128)(2,1)S(1)}, bf16[2,176,2048]{2,1,0:T(8,128)(2,1)}, u32[]{:S(2)}) copy-start(bf16[2,176,2048]{2,1,0:T(8,128)(2,1)} %param.27) | copy-start | bytes 4325380
  328.9 58.3 %copy-start.4 = (f32[128,6]{0,1:T(8,128)S(1)}, f32[128,6]{0,1:T(8,128)}, u32[]{:S(2)}) copy-start(f32[128,6]{0,1:T(8,128)} %param.25) | copy-start | bytes 9220
  377.1 32.9 %all-to-all-start.2 = ((bf16[32,2,24,256]{3,2,1,0:T(8,128)(2,1)}), bf16[32,2,24,256]{3,2,1,0:T(8,128)(2,1)}, u32[]{:S(2)}, u32[]{:S(2)}) async-start(bf16[32,2,24,256]{3,2,1,0:T(8,128)(2,1)} %copy.80), calls=%async_computation.4 | async-start | bytes 1572864 | tf_op jit(solution)/shard_map/all_to_all | solution.py:198
  413.3 2.7 copy-start.1
Sparse Core Ops, SparseCore 0:
  11.1 79.7 all-gather.6
  189.4 31.9 reduce-scatter.2
  277.9 40.6 all-gather.4
  329.0 45.9 reduce-scatter.4

commit v2 on v1

--- a/solution.py
+++ b/solution.py
@@ -24,52 +24,67 @@
     return hi, mid, lo
 
 
-def shard_kernel(q_ref, k_ref, v_ref, o_ref, st_ref, *, score_scale):
+def shard_kernel(flag_ref, q_ref, k_ref, v_ref, o_ref, st_ref, *, score_scale):
+    step = pl.program_id(0)
     blocks, rows, width = q_ref.shape
-    q = q_ref[...].reshape(blocks * rows, width)
-    scores = (
-        lax.dot_general(
-            q, k_ref[...], (((1,), (1,)), ((), ())), preferred_element_type=jnp.float32
-        )
-        * score_scale
-    )
-    shift = jnp.max(scores, axis=1, keepdims=True)
-    weights = jnp.exp(scores - shift)
-    total = jnp.sum(weights, axis=1, keepdims=True)
-    gathered = jnp.dot(
-        weights.astype(jnp.bfloat16), v_ref[...], preferred_element_type=jnp.float32
-    )
-    o_ref[...] = gathered.astype(jnp.bfloat16).reshape(blocks, 1, rows, width)
-    parts = split3(shift) + split3(total)
-    for col, part in enumerate(parts):
-        st_ref[0, :, col : col + 1] = part
-    st_ref[0, :, 6:8] = jnp.zeros((blocks * rows, 2), jnp.float32)
-
-
-def shard_attention(gathered_q, keys, values, score_scale):
+    for i in range(blocks):
+        present = flag_ref[step * blocks + i] > 0
+
+        @pl.when(present)
+        def _():
+            scores = (
+                lax.dot_general(
+                    q_ref[i], k_ref[...], (((1,), (1,)), ((), ())),
+                    preferred_element_type=jnp.float32,
+                )
+                * score_scale
+            )
+            shift = jnp.max(scores, axis=1, keepdims=True)
+            weights = jnp.exp(scores - shift)
+            total = jnp.sum(weights, axis=1, keepdims=True)
+            gathered = jnp.dot(
+                weights.astype(jnp.bfloat16), v_ref[...], preferred_element_type=jnp.float32
+            )
+            o_ref[i, 0] = gathered.astype(jnp.bfloat16)
+            parts = split3(shift) + split3(total)
+            for col, part in enumerate(parts):
+                st_ref[0, i * rows : (i + 1) * rows, col : col + 1] = part
+            st_ref[0, i * rows : (i + 1) * rows, 6:8] = jnp.zeros((rows, 2), jnp.float32)
+
+        @pl.when(jnp.logical_not(present))
+        def _():
+            o_ref[i, 0] = jnp.zeros((rows, width), jnp.bfloat16)
+            st_ref[0, i * rows : (i + 1) * rows, :] = jnp.zeros((rows, 8), jnp.float32)
+
+
+def shard_attention(flags, gathered_q, keys, values, score_scale):
     sources, padded_rows, two_heads = gathered_q.shape
     head_size = keys.shape[1]
     rows = padded_rows - 1
     heads = two_heads // head_size
     tb = TOKEN_BLOCKS
     kernel = functools.partial(shard_kernel, score_scale=score_scale)
+    grid_spec = pltpu.PrefetchScalarGridSpec(
+        num_scalar_prefetch=1,
+        grid=(sources // tb, heads),
+        in_specs=[
+            pl.BlockSpec((tb, rows, head_size), lambda b, h, f: (b, 0, h)),
+            pl.BlockSpec(keys.shape, lambda b, h, f: (0, 0)),
+            pl.BlockSpec(values.shape, lambda b, h, f: (0, 0)),
+        ],
+        out_specs=[
+            pl.BlockSpec((tb, 1, rows, head_size), lambda b, h, f: (b, h, 0, 0)),
+            pl.BlockSpec((1, tb * rows, 8), lambda b, h, f: (h, b, 0)),
+        ],
+    )
     return pl.pallas_call(
         kernel,
-        grid=(sources // tb, heads),
-        in_specs=[
-            pl.BlockSpec((tb, rows, head_size), lambda b, h: (b, 0, h)),
-            pl.BlockSpec(keys.shape, lambda b, h: (0, 0)),
-            pl.BlockSpec(values.shape, lambda b, h: (0, 0)),
-        ],
-        out_specs=[
-            pl.BlockSpec((tb, 1, rows, head_size), lambda b, h: (b, h, 0, 0)),
-            pl.BlockSpec((1, tb * rows, 8), lambda b, h: (h, b, 0)),
-        ],
+        grid_spec=grid_spec,
         out_shape=[
             jax.ShapeDtypeStruct((sources, heads, rows, head_size), jnp.bfloat16),
             jax.ShapeDtypeStruct((heads, sources * rows, 8), jnp.float32),
         ],
-    )(gathered_q, keys, values)
+    )(flags, gathered_q, keys, values)
 
 
 def body(
@@ -101,15 +116,18 @@
     prefix_row = jnp.zeros((1, query.shape[1]), jnp.bfloat16).at[0, :tok_rows].set(
         row_prefix.astype(jnp.bfloat16)
     )
-    gathered_q = lax.all_gather(
-        jnp.concatenate([query, prefix_row], axis=0), "seq", axis=0, tiled=False
-    )
-    sources = gathered_q.shape[0]
+    own_rows = jnp.concatenate([query, prefix_row], axis=0)
+    sources = lax.axis_size("seq")
+    gathered_q = lax.all_to_all(
+        jnp.broadcast_to(own_rows[None], (sources,) + own_rows.shape),
+        "seq", split_axis=0, concat_axis=0, tiled=True,
+    )
     own_cache = lax.dynamic_slice_in_dim(prefix_kv, kv_head, 1, 1)[:, 0]
+    valid = gathered_q[:, tok_rows, :tok_rows] == shard_prefix[0].astype(jnp.bfloat16)
+    flags = jnp.any(valid, axis=1).astype(jnp.int32)
     part_o, part_st = shard_attention(
-        gathered_q, own_cache[:, 0], own_cache[:, 1], score_scale
-    )
-    valid = gathered_q[:, tok_rows, :tok_rows] == shard_prefix[0].astype(jnp.bfloat16)
+        flags, gathered_q, own_cache[:, 0], own_cache[:, 1], score_scale
+    )
     stats = part_st.reshape(heads_here, sources, tok_rows, 8)
     keep = valid[None, :, :, None]
     column = jnp.arange(8)[None, None, None, :]
@@ -151,7 +169,14 @@
     model_width = residual.shape[1]
     slice_width = model_width // lax.axis_size("tensor")
     first_col = lax.axis_index("tensor") * slice_width
-    shared = lax.psum_scatter(projected, "tensor", scatter_dimension=1, tiled=True)
+    tensor_size = lax.axis_size("tensor")
+    shared = jnp.sum(
+        lax.all_to_all(
+            projected.reshape(tok_rows, tensor_size, slice_width),
+            "tensor", split_axis=1, concat_axis=1, tiled=True,
+        ),
+        axis=1,
+    )
     hidden_state = (
         lax.dynamic_slice_in_dim(residual, first_col, slice_width, 1).astype(jnp.float32) + shared
     )

time: 425 us -> 406 us (0.955)
  waiting for transfers between devices: 261 us -> 218 us
  starting transfers between devices: 17.7 us -> 33 us
  Pallas kernels: 29.1 us -> 34.5 us
    all_gather x1 -> x0, waiting for transfers between devices: 76.8 us -> none  [body(): lax.all_gather(jnp.concatenate([query, prefix_row], axis=0), 'seq', axis=...]
    all_to_all x0 -> x2, waiting for transfers between devices: none -> 60.9 us  [the longest x1 48.7 us: body(): lax.all_to_all(jnp.broadcast_to(own_rows[None], (sources,) + own_rows.sha...]
    reduce_scatter x1 -> x0, waiting for transfers between devices: 28.3 us -> none  [body(): lax.psum_scatter(projected, 'tensor', scatter_dimension=1, tiled=True)]
    all_to_all x0 -> x2, starting transfers between devices: none -> 15.7 us  [the longest x1 11.4 us: body(): lax.all_to_all(jnp.broadcast_to(own_rows[None], (sources,) + own_rows.sha...]
    pallas_call x1, Pallas kernels: 29.1 us -> 34.5 us  [shard_attention(): pl.pallas_call(kernel, grid_spec=grid_spec, out_shape=[jax.ShapeDtypeStru...]
where the time goes in v2:
time: 406 us; the launch traced here: 405 us
  waiting for transfers between devices  218 us (54%)
  blocking collectives  43.2 us (11%)
  Pallas kernels  34.5 us (8%)
  starting transfers between devices  33 us (8%)
  local copies, waits for them, and re-layouts  26.6 us (7%)
  other arithmetic  21.1 us (5%)
  between operations  15 us (4%)
  matrix products  13.3 us (3%)
    all_to_all x1, waiting for transfers between devices, body(): lax.all_to_all(jnp.broadcast_to(own_rows[None], (sources,) + own_rows.sha...  48.7 us
    all_to_all x1, waiting for transfers between devices, body(): lax.all_to_all(outgoing, 'seq', split_axis=0, concat_axis=0, tiled=True)  48.2 us
    reduce_scatter x1, waiting for transfers between devices, body(): lax.psum_scatter(group_terms.astype(jnp.bfloat16), 'tensor', scatter_dime...  46.1 us
    all_gather x1, waiting for transfers between devices, body(): lax.all_gather(incoming, 'tensor', axis=3, tiled=True)  40.6 us
    pallas_call x1, Pallas kernels, shard_attention(): pl.pallas_call(kernel, grid_spec=grid_spec, out_shape=[jax.ShapeDtypeStru...  34.5 us
    all_to_all x1, blocking collectives, body(): lax.all_to_all(outgoing.reshape(sources, exp_here, capacity, slice_width)...  30.5 us
    all_to_all x1, waiting for transfers between devices, body(): lax.all_to_all(expert_rows_out, 'seq', split_axis=0, concat_axis=0, tiled...  22.6 us
    psum x1, blocking collectives, body(): squares = lax.psum(jnp.sum(hidden_state * hidden_state, axis=1), 'tensor')  12.7 us
  transfers between devices with their start and end apart: 6, of which 6 were waited for; matrix products, arithmetic and copies ran while one was open for 2% of the time, Pallas kernels for 0%

profile of v2, /device:TPU:32, one launch (start us, length us, event | category | flops | bytes accessed | tf_op | source)
XLA Modules:
  0.0 405.4 jit_solution(9045091110141190920)
XLA Ops:
  7.8 1.0 select_reduce_fusion
  10.3 1.5 broadcast_in_dim.83
  11.8 11.4 %all-to-all-start = ((bf16[32,129,256]{2,1,0:T(8,128)(2,1)}), bf16[32,129,256]{2,1,0:T(8,128)(2,1)}, u32[]{:S(2)}, u32[]{:S(2)}) async-start(bf16[32,129,256]{2,1,0:T(8,128)(2,1)} %broadcast_in_dim.83), calls=%async_computation | async-start | bytes 4456448 | tf_op jit(solution)/shard_map/all_to_all | solution.py:121
  23.3 1.4 constant_dynamic-slice_fusion.1
  26.3 48.7 %all-to-all-done.q_ref = bf16[32,129,256]{2,1,0:T(8,128)(2,1)} async-done(((bf16[32,129,256]{2,1,0:T(8,128)(2,1)}), bf16[32,129,256]{2,1,0:T(8,128)(2,1)}, u32[]{:S(2)}, u32[]{:S(2)}) %all-to-all-start) | async-done | bytes 2113568 | tf_op jit(solution)/shard_map/all_to_all | solution.py:121
  74.9 1.5 fusion.44
  77.0 34.5 %shard_map.140 = (bf16[32,2,128,128]{3,2,1,0:T(8,128)(2,1)}, f32[2,4096,8]{2,1,0:T(8,128)}) custom-call(s32[32]{0:T(128)} %convert_element_type.75.flag_ref, bf16[32,129,256]{2,1,0:T(8,128)(2,1)} %all-to-all-done.q_ref, bf16[1024,128]{1,0:T(8,128)(2,1)} %get-tuple-element.27.k_ref, bf16[1024,128]{1,0:T(8,128)(2,1)} %get-tuple-element.26.v_ref), custom_call_target="tpu_custom_call" | custom-call | tf_op jit(solution)/shard_map/pallas_call | solution.py:80
  111.5 2.5 copy.68
  114.1 3.2 pad_maximum_fusion
  117.3 6.9 %all-to-all-start.1 = ((bf16[32,2,136,128]{3,2,1,0:T(8,128)(2,1)}), bf16[32,2,136,128]{3,2,1,0:T(8,128)(2,1)}, u32[]{:S(2)}, u32[]{:S(2)}) async-start(bf16[32,2,136,128]{3,2,1,0:T(8,128)(2,1)} %pad_maximum_fusion), calls=%async_computation.1 | async-start | bytes 4456448 | tf_op jit(solution)/shard_map/all_to_all | solution.py:137
  125.2 2.3 copy.95
  127.8 48.2 %all-to-all-done.1 = bf16[32,2,136,128]{3,2,1,0:T(8,128)(2,1)} async-done(((bf16[32,2,136,128]{3,2,1,0:T(8,128)(2,1)}), bf16[32,2,136,128]{3,2,1,0:T(8,128)(2,1)}, u32[]{:S(2)}, u32[]{:S(2)}) %all-to-all-start.1) | async-done | bytes 2228256 | tf_op jit(solution)/shard_map/all_to_all | solution.py:137
  177.2 3.1 multiply_reduce_fusion
  180.7 2.7 fusion.47
  183.4 4.3 %all-to-all-start.2 = ((f32[128,8,256]{2,0,1:T(8,128)}), f32[128,8,256]{2,0,1:T(8,128)}, u32[]{:S(2)}, u32[]{:S(2)}) async-start(f32[128,8,256]{2,0,1:T(8,128)} %fusion.47), calls=%async_computation.2 | async-start | bytes 2097152 | tf_op jit(solution)/shard_map/all_to_all | solution.py:174
  188.2 1.8 reduce-window.6
  191.5 12.3 %all-to-all-done.2 = f32[128,8,256]{2,0,1:T(8,128)} async-done(((f32[128,8,256]{2,0,1:T(8,128)}), f32[128,8,256]{2,0,1:T(8,128)}, u32[]{:S(2)}, u32[]{:S(2)}) %all-to-all-start.2) | async-done | bytes 1048608 | tf_op jit(solution)/shard_map/all_to_all | solution.py:174
  203.7 1.3 reduce_sum.87
  206.0 12.7 %psum.7 = f32[128]{0:T(128)S(1)} all-reduce(f32[128]{0:T(128)S(1)} %multiply_reduce_fusion.2), channel_id=1, replica_groups=mesh['seq'=32,'tensor'=8] {'tensor'}, use_global_device_ids=true, to_apply=%region_13.14 | all-reduce | flops 128 | bytes 1024 | tf_op jit(solution)/shard_map/psum | solution.py:183
  220.6 6.7 %scatter_custom_fusion = bf16[1536,256]{1,0:T(8,128)(2,1)} fusion(s32[768]{0:T(1024)S(1)} %fusion.35, bf16[768,256]{1,0:T(8,128)(2,1)} %reshape.244, bf16[]{:T(256)} %constant.72.clone.1), kind=kCustom, calls=%fused_computation.25 | custom fusion | bytes 786944 | tf_op jit(solution)/shard_map/scatter | solution.py:201
  227.3 30.5 %all_to_all.25 = bf16[32,2,24,256]{3,2,1,0:T(8,128)(2,1)S(1)} all-to-all(bf16[32,2,24,256]{3,2,1,0:T(8,128)(2,1)} %bitcast.142), channel_id=1, replica_groups=mesh['seq'=32,'tensor'=8] {'seq'}, dimensions={0} | all-to-all | bytes 1572864 | tf_op jit(solution)/shard_map/all_to_all | solution.py:203
  259.0 40.6 %all-gather.2.cloned.1.call-done = bf16[32,2,24,2048]{3,2,0,1:T(8,128)(2,1)} async-done(((bf16[32,2,24,256]{3,2,0,1:T(8,128)(2,1)}), bf16[32,2,24,2048]{3,2,0,1:T(8,128)(2,1)}) %all-gather.2.cloned.1.call-update) | async-done | bytes 6291472 | tf_op jit(solution)/shard_map/all_gather | solution.py:212
  299.6 5.7 %fusion.3 = f32[32,2,24,2,176]{4,2,3,0,1:T(8,128)S(1)} fusion(bf16[2,2048,2,176]{1,3,2,0:T(8,128)(2,1)S(1)} %copy-done, bf16[32,2,24,2048]{3,2,0,1:T(8,128)(2,1)} %all-gather.2.cloned.1.call-done), kind=kOutput, calls=%fused_computation.8 | convolution fusion | flops 2214592512 | bytes 11337728 | tf_op jit(solution)/shard_map/sjcd,jdgh->sjcgh/dot_general | solution.py:210
  305.3 4.6 %convert_bitcast_fusion = bf16[32,2,24,2048]{3,2,0,1:T(8,128)(2,1)} fusion(bf16[2,176,2048]{2,1,0:T(8,128)(2,1)S(1)} %copy-done.5, f32[32,2,24,2,176]{4,2,3,0,1:T(8,128)S(1)} %fusion.3), kind=kOutput, calls=%fused_computation.4 | convolution fusion | flops 1112064000 | bytes 9895936 | tf_op jit(solution)/shard_map/sjch,jhd->sjcd/dot_general | solution.py:217
  309.9 46.1 %reduce-scatter.2.cloned.1.call-done = bf16[32,2,24,256]{3,2,0,1:T(8,128)(2,1)} async-done(((bf16[32,2,24,2048]{3,2,0,1:T(8,128)(2,1)}), bf16[32,2,24,256]{3,2,0,1:T(8,128)(2,1)}) %reduce-scatter.2.cloned.1.call-update) | async-done | bytes 786448 | tf_op jit(solution)/shard_map/reduce_scatter | solution.py:220
  356.1 2.1 copy.86
  358.1 10.1 %all-to-all-start.4 = ((bf16[32,2,24,256]{3,2,1,0:T(8,128)(2,1)}), bf16[32,2,24,256]{3,2,1,0:T(8,128)(2,1)}, u32[]{:S(2)}, u32[]{:S(2)}) async-start(bf16[32,2,24,256]{3,2,1,0:T(8,128)(2,1)} %copy.86), calls=%async_computation.5 | async-start | bytes 1572864 | tf_op jit(solution)/shard_map/all_to_all | solution.py:223
  368.4 22.6 %all-to-all-done.4 = bf16[32,2,24,256]{3,2,1,0:T(8,128)(2,1)} async-done(((bf16[32,2,24,256]{3,2,1,0:T(8,128)(2,1)}), bf16[32,2,24,256]{3,2,1,0:T(8,128)(2,1)}, u32[]{:S(2)}, u32[]{:S(2)}) %all-to-all-start.4) | async-done | bytes 786464 | tf_op jit(solution)/shard_map/all_to_all | solution.py:223
  391.0 3.3 gather_fusion
  394.3 1.1 reshape.231
  395.4 1.6 multiply_reduce_fusion.1
  397.0 1.5 add_convert_fusion
  (58 shorter events, 12.5 us)
Async XLA Ops:
  7.2 292.5 %copy-start = (bf16[2,2048,2,176]{1,3,2,0:T(8,128)(2,1)S(1)}, bf16[2,2048,2,176]{1,3,2,0:T(8,128)(2,1)}, u32[]{:S(2)}) copy-start(bf16[2,2048,2,176]{1,3,2,0:T(8,128)(2,1)} %param.26) | copy-start | bytes 8650756
  11.8 63.1 %all-to-all-start = ((bf16[32,129,256]{2,1,0:T(8,128)(2,1)}), bf16[32,129,256]{2,1,0:T(8,128)(2,1)}, u32[]{:S(2)}, u32[]{:S(2)}) async-start(bf16[32,129,256]{2,1,0:T(8,128)(2,1)} %broadcast_in_dim.83), calls=%async_computation | async-start | bytes 4456448 | tf_op jit(solution)/shard_map/all_to_all | solution.py:121
  117.3 58.7 %all-to-all-start.1 = ((bf16[32,2,136,128]{3,2,1,0:T(8,128)(2,1)}), bf16[32,2,136,128]{3,2,1,0:T(8,128)(2,1)}, u32[]{:S(2)}, u32[]{:S(2)}) async-start(bf16[32,2,136,128]{3,2,1,0:T(8,128)(2,1)} %pad_maximum_fusion), calls=%async_computation.1 | async-start | bytes 4456448 | tf_op jit(solution)/shard_map/all_to_all | solution.py:137
  124.3 3.2 copy-start.4
  124.3 3.3 copy-start.1
  180.7 7.0 %copy-start.2 = (s32[128,6]{0,1:T(8,128)S(1)}, s32[128,6]{0,1:T(8,128)}, u32[]{:S(2)}) copy-start(s32[128,6]{0,1:T(8,128)} %param.24) | copy-start | bytes 9220
  183.4 20.3 %all-to-all-start.2 = ((f32[128,8,256]{2,0,1:T(8,128)}), f32[128,8,256]{2,0,1:T(8,128)}, u32[]{:S(2)}, u32[]{:S(2)}) async-start(f32[128,8,256]{2,0,1:T(8,128)} %fusion.47), calls=%async_computation.2 | async-start | bytes 2097152 | tf_op jit(solution)/shard_map/all_to_all | solution.py:174
  187.7 111.9 %all-gather.2.cloned.1.call-start = ((), (), s32[]{:S(2)}) async-start(), calls=%async_computation.6 | async-start | bytes 7077888 | tf_op jit(solution)/shard_map/all_gather | solution.py:212
  258.8 97.3 %reduce-scatter.2.cloned.1.call-start = ((), (), s32[]{:S(2)}) async-start(), calls=%async_computation.7 | async-start | bytes 7077888 | tf_op jit(solution)/shard_map/reduce_scatter | solution.py:220
  299.6 5.7 %copy-start.5 = (bf16[2,176,2048]{2,1,0:T(8,128)(2,1)S(1)}, bf16[2,176,2048]{2,1,0:T(8,128)(2,1)}, u32[]{:S(2)}) copy-start(bf16[2,176,2048]{2,1,0:T(8,128)(2,1)} %param.27) | copy-start | bytes 4325380
  309.9 58.4 %copy-start.3 = (f32[128,6]{0,1:T(8,128)S(1)}, f32[128,6]{0,1:T(8,128)}, u32[]{:S(2)}) copy-start(f32[128,6]{0,1:T(8,128)} %param.25) | copy-start | bytes 9220
  358.1 32.8 %all-to-all-start.4 = ((bf16[32,2,24,256]{3,2,1,0:T(8,128)(2,1)}), bf16[32,2,24,256]{3,2,1,0:T(8,128)(2,1)}, u32[]{:S(2)}, u32[]{:S(2)}) async-start(bf16[32,2,24,256]{3,2,1,0:T(8,128)(2,1)} %copy.86), calls=%async_computation.5 | async-start | bytes 1572864 | tf_op jit(solution)/shard_map/all_to_all | solution.py:223
Sparse Core Ops, SparseCore 0:
  258.9 40.6 all-gather.1
  310.0 45.9 reduce-scatter.1

commit v3 on v2

--- a/solution.py
+++ b/solution.py
@@ -7,13 +7,14 @@
 from jax.experimental.pallas import tpu as pltpu
 from jax.sharding import PartitionSpec as P
 
+
 QH = 16
 KVH = 4
 
 
-NEG_FLOOR = -1e30
 NEG_SHIFT = -(2.0 ** 100)
 TOKEN_BLOCKS = 4
+STAT_ROWS = 16
 
 
 def split3(x):
@@ -24,9 +25,14 @@
     return hi, mid, lo
 
 
-def shard_kernel(flag_ref, q_ref, k_ref, v_ref, o_ref, st_ref, *, score_scale):
+def shard_kernel(flag_ref, q_ref, k_ref, v_ref, o_ref, *, score_scale):
     step = pl.program_id(0)
-    blocks, rows, width = q_ref.shape
+    blocks, padded_rows, width = q_ref.shape
+    rows = padded_rows - 1
+    stat_rows = o_ref.shape[2] - rows
+    owner = flag_ref[flag_ref.shape[0] - 1].astype(jnp.float32)
+    kind = lax.broadcasted_iota(jnp.int32, (stat_rows, width), 0)
+    blank = jnp.where(kind == 0, NEG_SHIFT, 0.0)
     for i in range(blocks):
         present = flag_ref[step * blocks + i] > 0
 
@@ -34,7 +40,7 @@
         def _():
             scores = (
                 lax.dot_general(
-                    q_ref[i], k_ref[...], (((1,), (1,)), ((), ())),
+                    q_ref[i, :rows, :], k_ref[...], (((1,), (1,)), ((), ())),
                     preferred_element_type=jnp.float32,
                 )
                 * score_scale
@@ -45,49 +51,44 @@
             gathered = jnp.dot(
                 weights.astype(jnp.bfloat16), v_ref[...], preferred_element_type=jnp.float32
             )
-            o_ref[i, 0] = gathered.astype(jnp.bfloat16)
-            parts = split3(shift) + split3(total)
-            for col, part in enumerate(parts):
-                st_ref[0, i * rows : (i + 1) * rows, col : col + 1] = part
-            st_ref[0, i * rows : (i + 1) * rows, 6:8] = jnp.zeros((rows, 2), jnp.float32)
+            o_ref[i, 0, :rows, :] = gathered.astype(jnp.bfloat16)
+            lane = lax.broadcasted_iota(jnp.int32, (rows, width), 1)
+            table = jnp.zeros((rows, width), jnp.float32)
+            for col, part in enumerate(split3(shift) + split3(total)):
+                table = jnp.where(lane == col, part, table)
+            table = jnp.transpose(table)[:stat_rows, :]
+            matching = q_ref[i, rows:, :].astype(jnp.float32) == owner
+            o_ref[i, 0, rows:, :] = jnp.where(matching, table, blank).astype(jnp.bfloat16)
 
         @pl.when(jnp.logical_not(present))
         def _():
-            o_ref[i, 0] = jnp.zeros((rows, width), jnp.bfloat16)
-            st_ref[0, i * rows : (i + 1) * rows, :] = jnp.zeros((rows, 8), jnp.float32)
+            o_ref[i, 0, :rows, :] = jnp.zeros((rows, width), jnp.bfloat16)
+            o_ref[i, 0, rows:, :] = blank.astype(jnp.bfloat16)
 
 
 def shard_attention(flags, gathered_q, keys, values, score_scale):
-    sources, padded_rows, two_heads = gathered_q.shape
-    head_size = keys.shape[1]
+    sources, padded_rows, head_size = gathered_q.shape
     rows = padded_rows - 1
-    heads = two_heads // head_size
     tb = TOKEN_BLOCKS
     kernel = functools.partial(shard_kernel, score_scale=score_scale)
     grid_spec = pltpu.PrefetchScalarGridSpec(
         num_scalar_prefetch=1,
-        grid=(sources // tb, heads),
+        grid=(sources // tb,),
         in_specs=[
-            pl.BlockSpec((tb, rows, head_size), lambda b, h, f: (b, 0, h)),
-            pl.BlockSpec(keys.shape, lambda b, h, f: (0, 0)),
-            pl.BlockSpec(values.shape, lambda b, h, f: (0, 0)),
+            pl.BlockSpec((tb, padded_rows, head_size), lambda b, f: (b, 0, 0)),
+            pl.BlockSpec(keys.shape, lambda b, f: (0, 0)),
+            pl.BlockSpec(values.shape, lambda b, f: (0, 0)),
         ],
-        out_specs=[
-            pl.BlockSpec((tb, 1, rows, head_size), lambda b, h, f: (b, h, 0, 0)),
-            pl.BlockSpec((1, tb * rows, 8), lambda b, h, f: (h, b, 0)),
-        ],
+        out_specs=pl.BlockSpec((tb, 1, rows + STAT_ROWS, head_size), lambda b, f: (b, 0, 0, 0)),
     )
     return pl.pallas_call(
         kernel,
         grid_spec=grid_spec,
-        out_shape=[
-            jax.ShapeDtypeStruct((sources, heads, rows, head_size), jnp.bfloat16),
-            jax.ShapeDtypeStruct((heads, sources * rows, 8), jnp.float32),
-        ],
+        out_shape=jax.ShapeDtypeStruct((sources, 1, rows + STAT_ROWS, head_size), jnp.bfloat16),
     )(flags, gathered_q, keys, values)
 
 
-def body(
+def layer(
     query,
     suffix_kv,
     segment_ids,
@@ -113,32 +114,37 @@
     row_prefix = jnp.sum(
         jnp.where(segments[:, None] == requests[None, :], request_prefix[0][None, :], 0), axis=1
     )
-    prefix_row = jnp.zeros((1, query.shape[1]), jnp.bfloat16).at[0, :tok_rows].set(
+    prefix_row = jnp.zeros((1, head_size), jnp.bfloat16).at[0, :tok_rows].set(
         row_prefix.astype(jnp.bfloat16)
     )
-    own_rows = jnp.concatenate([query, prefix_row], axis=0)
     sources = lax.axis_size("seq")
-    gathered_q = lax.all_to_all(
-        jnp.broadcast_to(own_rows[None], (sources,) + own_rows.shape),
-        "seq", split_axis=0, concat_axis=0, tiled=True,
-    )
     own_cache = lax.dynamic_slice_in_dim(prefix_kv, kv_head, 1, 1)[:, 0]
-    valid = gathered_q[:, tok_rows, :tok_rows] == shard_prefix[0].astype(jnp.bfloat16)
-    flags = jnp.any(valid, axis=1).astype(jnp.int32)
-    part_o, part_st = shard_attention(
-        flags, gathered_q, own_cache[:, 0], own_cache[:, 1], score_scale
-    )
-    stats = part_st.reshape(heads_here, sources, tok_rows, 8)
-    keep = valid[None, :, :, None]
-    column = jnp.arange(8)[None, None, None, :]
-    stats = jnp.where(keep, stats, jnp.where(column == 0, NEG_SHIFT, 0.0))
-    stats = jnp.transpose(stats, (1, 0, 3, 2)).astype(jnp.bfloat16)
-    outgoing = jnp.concatenate([part_o, stats], axis=2)
-    returned = lax.all_to_all(outgoing, "seq", split_axis=0, concat_axis=0, tiled=True)
-    got_o = returned[:, :, :tok_rows, :].astype(jnp.float32)
-    got_st = returned[:, :, tok_rows:, :].astype(jnp.float32)
-    got_shift = got_st[:, :, 0] + got_st[:, :, 1] + got_st[:, :, 2]
-    got_total = got_st[:, :, 3] + got_st[:, :, 4] + got_st[:, :, 5]
+    got_o, got_shift, got_total = [], [], []
+    flags = None
+    for head in range(heads_here):
+        own_rows = jnp.concatenate(
+            [query[:, head * head_size : (head + 1) * head_size], prefix_row], axis=0
+        )
+        gathered_q = lax.all_to_all(
+            jnp.broadcast_to(own_rows[None], (sources,) + own_rows.shape),
+            "seq", split_axis=0, concat_axis=0, tiled=True,
+        )
+        if flags is None:
+            valid = gathered_q[:, tok_rows, :tok_rows] == shard_prefix[0].astype(jnp.bfloat16)
+            flags = jnp.concatenate(
+                [jnp.any(valid, axis=1).astype(jnp.int32), shard_prefix.astype(jnp.int32)]
+            )
+        outgoing = shard_attention(flags, gathered_q, own_cache[:, 0], own_cache[:, 1], score_scale)
+        returned = lax.all_to_all(
+            outgoing, "seq", split_axis=0, concat_axis=0, tiled=True
+        )
+        got_st = returned[:, 0, tok_rows:, :].astype(jnp.float32)
+        got_o.append(returned[:, 0, :tok_rows, :].astype(jnp.float32))
+        got_shift.append(got_st[:, 0] + got_st[:, 1] + got_st[:, 2])
+        got_total.append(got_st[:, 3] + got_st[:, 4] + got_st[:, 5])
+    got_o = jnp.stack(got_o, axis=1)
+    got_shift = jnp.stack(got_shift, axis=1)
+    got_total = jnp.stack(got_total, axis=1)
 
     own_suffix = lax.dynamic_slice_in_dim(suffix_kv, kv_head, 1, 1).reshape(tok_rows, 2, head_size)
     positions = jnp.arange(tok_rows)
@@ -246,4 +252,4 @@
         P("seq", "tensor", None),
     )
     out_specs = (P("seq", "tensor"), P("seq", "tensor"))
-    return jax.shard_map(body, mesh=mesh, in_specs=in_specs, out_specs=out_specs, check_vma=False)
+    return jax.shard_map(layer, mesh=mesh, in_specs=in_specs, out_specs=out_specs, check_vma=False)

time: 406 us -> 388 us (0.956)
  waiting for transfers between devices: 218 us -> 168 us
  blocking collectives: 43.2 us -> 83.2 us
  other arithmetic: 21.1 us -> 14.7 us
    all_to_all x4 -> x5, waiting for transfers between devices: 132 us -> 80.6 us  [the longest x2 39.2 us: layer(): lax.all_to_all(outgoing, 'seq', split_axis=0, concat_axis=0, tiled=True)]
    all_to_all x1 -> x2, blocking collectives: 30.5 us -> 70.3 us  [the longest x1 42.1 us: layer(): lax.all_to_all(jnp.broadcast_to(own_rows[None], (sources,) + own_rows.sha...]
    all_to_all x4 -> x5, starting transfers between devices: 32.7 us -> 30.5 us  [the longest x2 10.6 us: layer(): lax.all_to_all(outgoing, 'seq', split_axis=0, concat_axis=0, tiled=True)]
    pallas_call x1 -> x2, Pallas kernels: 34.5 us -> 34.5 us  [shard_attention(): pl.pallas_call(kernel, grid_spec=grid_spec, out_shape=jax.ShapeDtypeStruc...]
  transfers between devices with their start and end apart: 6 -> 7, of which waited for: 6 -> 7; matrix products, arithmetic and copies ran while one was open for 2% -> 3% of each run, Pallas kernels for 0% -> 9%
where the time goes in v3:
time: 388 us; the launch traced here: 386 us
  waiting for transfers between devices  168 us (43%)
  blocking collectives  83.2 us (21%)
  Pallas kernels  34.5 us (9%)
  starting transfers between devices  30.6 us (8%)
  local copies, waits for them, and re-layouts  27.3 us (7%)
  between operations  15 us (4%)
  other arithmetic  14.7 us (4%)
  matrix products  13.3 us (3%)
    reduce_scatter x1, waiting for transfers between devices, layer(): lax.psum_scatter(group_terms.astype(jnp.bfloat16), 'tensor', scatter_dime...  46.1 us
    all_to_all x1, blocking collectives, layer(): lax.all_to_all(jnp.broadcast_to(own_rows[None], (sources,) + own_rows.sha...  42.1 us
    all_gather x1, waiting for transfers between devices, layer(): lax.all_gather(incoming, 'tensor', axis=3, tiled=True)  40.8 us
    all_to_all x2, waiting for transfers between devices, layer(): lax.all_to_all(outgoing, 'seq', split_axis=0, concat_axis=0, tiled=True)  39.2 us
    pallas_call x2, Pallas kernels, shard_attention(): pl.pallas_call(kernel, grid_spec=grid_spec, out_shape=jax.ShapeDtypeStruc...  34.5 us
    all_to_all x1, blocking collectives, layer(): lax.all_to_all(outgoing.reshape(sources, exp_here, capacity, slice_width)...  28.2 us
    all_to_all x1, waiting for transfers between devices, layer(): lax.all_to_all(expert_rows_out, 'seq', split_axis=0, concat_axis=0, tiled...  22.6 us
    psum x1, blocking collectives, layer(): squares = lax.psum(jnp.sum(hidden_state * hidden_state, axis=1), 'tensor')  12.9 us
  transfers between devices with their start and end apart: 7, of which 7 were waited for; matrix products, arithmetic and copies ran while one was open for 3% of the time, Pallas kernels for 9%

profile of v3, /device:TPU:32, one launch (start us, length us, event | category | flops | bytes accessed | tf_op | source)
XLA Modules:
  0.0 386.2 jit_solution(5884028249264123708)
XLA Ops:
  9.0 42.1 %all_to_all.35.q_ref = bf16[32,129,128]{2,1,0:T(8,128)(2,1)} all-to-all(bf16[32,129,128]{2,1,0:T(8,128)(2,1)S(1)} %broadcast_in_dim.37), channel_id=1, replica_groups=mesh['seq'=32,'tensor'=8] {'seq'}, dimensions={0} | all-to-all | bytes 2113536 | tf_op jit(solution)/shard_map/all_to_all | solution.py:128
  52.3 5.3 %all-to-all-start.2 = ((bf16[32,129,128]{2,1,0:T(8,128)(2,1)}), bf16[32,129,128]{2,1,0:T(8,128)(2,1)}, u32[]{:S(2)}, u32[]{:S(2)}) async-start(bf16[32,129,128]{2,1,0:T(8,128)(2,1)} %broadcast_in_dim.38), calls=%async_computation.2 | async-start | bytes 2228224 | tf_op jit(solution)/shard_map/all_to_all | solution.py:128
  57.6 1.4 constant_dynamic-slice_fusion.1
  60.6 1.5 compare_reduce_fusion
  62.7 17.2 %shard_map.140 = bf16[32,1,144,128]{3,2,1,0:T(8,128)(2,1)} custom-call(s32[33]{0:T(128)} %pad_add_fusion.flag_ref, bf16[32,129,128]{2,1,0:T(8,128)(2,1)} %all_to_all.35.q_ref, bf16[1024,128]{1,0:T(8,128)(2,1)} %get-tuple-element.21.k_ref, bf16[1024,128]{1,0:T(8,128)(2,1)} %get-tuple-element.20.v_ref), custom_call_target="tpu_custom_call" | custom-call | tf_op jit(solution)/shard_map/pallas_call | solution.py:84
  80.0 6.6 %all-to-all-done.2.q_ref = bf16[32,129,128]{2,1,0:T(8,128)(2,1)} async-done(((bf16[32,129,128]{2,1,0:T(8,128)(2,1)}), bf16[32,129,128]{2,1,0:T(8,128)(2,1)}, u32[]{:S(2)}, u32[]{:S(2)}) %all-to-all-start.2) | async-done | bytes 1056800 | tf_op jit(solution)/shard_map/all_to_all | solution.py:128
  86.6 5.2 %all-to-all-start.1 = ((bf16[32,1,144,128]{3,2,1,0:T(8,128)(2,1)}), bf16[32,1,144,128]{3,2,1,0:T(8,128)(2,1)}, u32[]{:S(2)}, u32[]{:S(2)}) async-start(bf16[32,1,144,128]{3,2,1,0:T(8,128)(2,1)} %shard_map.140), calls=%async_computation.1 | async-start | bytes 2359296 | tf_op jit(solution)/shard_map/all_to_all | solution.py:138
  91.8 17.3 %shard_map.141 = bf16[32,1,144,128]{3,2,1,0:T(8,128)(2,1)} custom-call(s32[33]{0:T(128)} %pad_add_fusion.flag_ref, bf16[32,129,128]{2,1,0:T(8,128)(2,1)} %all-to-all-done.2.q_ref, bf16[1024,128]{1,0:T(8,128)(2,1)} %get-tuple-element.21.k_ref, bf16[1024,128]{1,0:T(8,128)(2,1)} %get-tuple-element.20.v_ref), custom_call_target="tpu_custom_call" | custom-call | tf_op jit(solution)/shard_map/pallas_call | solution.py:84
  109.1 13.1 %all-to-all-done.1 = bf16[32,1,144,128]{3,2,1,0:T(8,128)(2,1)} async-done(((bf16[32,1,144,128]{3,2,1,0:T(8,128)(2,1)}), bf16[32,1,144,128]{3,2,1,0:T(8,128)(2,1)}, u32[]{:S(2)}, u32[]{:S(2)}) %all-to-all-start.1) | async-done | bytes 1179680 | tf_op jit(solution)/shard_map/all_to_all | solution.py:138
  122.1 5.4 %all-to-all-start.3 = ((bf16[32,1,144,128]{3,2,1,0:T(8,128)(2,1)}), bf16[32,1,144,128]{3,2,1,0:T(8,128)(2,1)}, u32[]{:S(2)}, u32[]{:S(2)}) async-start(bf16[32,1,144,128]{3,2,1,0:T(8,128)(2,1)} %shard_map.141), calls=%async_computation.3 | async-start | bytes 2359296 | tf_op jit(solution)/shard_map/all_to_all | solution.py:138
  128.5 2.3 copy.89
  132.1 26.1 %all-to-all-done.3 = bf16[32,1,144,128]{3,2,1,0:T(8,128)(2,1)} async-done(((bf16[32,1,144,128]{3,2,1,0:T(8,128)(2,1)}), bf16[32,1,144,128]{3,2,1,0:T(8,128)(2,1)}, u32[]{:S(2)}, u32[]{:S(2)}) %all-to-all-start.3) | async-done | bytes 1179680 | tf_op jit(solution)/shard_map/all_to_all | solution.py:138
  159.4 1.3 slice.129
  160.7 1.3 slice.130
  163.6 2.7 fusion.43
  166.3 4.4 %all-to-all-start.4 = ((f32[128,8,256]{2,0,1:T(8,128)}), f32[128,8,256]{2,0,1:T(8,128)}, u32[]{:S(2)}, u32[]{:S(2)}) async-start(f32[128,8,256]{2,0,1:T(8,128)} %fusion.43), calls=%async_computation.4 | async-start | bytes 2097152 | tf_op jit(solution)/shard_map/all_to_all | solution.py:180
  171.2 1.8 reduce-window.6
  174.5 12.3 %all-to-all-done.4 = f32[128,8,256]{2,0,1:T(8,128)} async-done(((f32[128,8,256]{2,0,1:T(8,128)}), f32[128,8,256]{2,0,1:T(8,128)}, u32[]{:S(2)}, u32[]{:S(2)}) %all-to-all-start.4) | async-done | bytes 1048608 | tf_op jit(solution)/shard_map/all_to_all | solution.py:180
  186.7 1.3 reduce_sum.87
  189.0 12.9 %psum.7 = f32[128]{0:T(128)S(1)} all-reduce(f32[128]{0:T(128)S(1)} %multiply_reduce_fusion.2), channel_id=1, replica_groups=mesh['seq'=32,'tensor'=8] {'tensor'}, use_global_device_ids=true, to_apply=%region_12.13 | all-reduce | flops 128 | bytes 1024 | tf_op jit(solution)/shard_map/psum | solution.py:189
  203.8 6.7 %scatter_custom_fusion = bf16[1536,256]{1,0:T(8,128)(2,1)} fusion(s32[768]{0:T(1024)S(1)} %fusion.35, bf16[768,256]{1,0:T(8,128)(2,1)} %reshape.221, bf16[]{:T(256)} %constant.76.clone.1), kind=kCustom, calls=%fused_computation.24 | custom fusion | bytes 786944 | tf_op jit(solution)/shard_map/scatter | solution.py:207
  210.5 28.2 %all_to_all.36 = bf16[32,2,24,256]{3,2,1,0:T(8,128)(2,1)S(1)} all-to-all(bf16[32,2,24,256]{3,2,1,0:T(8,128)(2,1)} %bitcast.137), channel_id=1, replica_groups=mesh['seq'=32,'tensor'=8] {'seq'}, dimensions={0} | all-to-all | bytes 1572864 | tf_op jit(solution)/shard_map/all_to_all | solution.py:209
  239.7 40.8 %all-gather.2.cloned.1.call-done = bf16[32,2,24,2048]{3,2,0,1:T(8,128)(2,1)} async-done(((bf16[32,2,24,256]{3,2,0,1:T(8,128)(2,1)}), bf16[32,2,24,2048]{3,2,0,1:T(8,128)(2,1)}) %all-gather.2.cloned.1.call-update) | async-done | bytes 6291472 | tf_op jit(solution)/shard_map/all_gather | solution.py:218
  280.5 5.7 %fusion.3 = f32[32,2,24,2,176]{4,2,3,0,1:T(8,128)S(1)} fusion(bf16[2,2048,2,176]{1,3,2,0:T(8,128)(2,1)S(1)} %copy-done, bf16[32,2,24,2048]{3,2,0,1:T(8,128)(2,1)} %all-gather.2.cloned.1.call-done), kind=kOutput, calls=%fused_computation.7 | convolution fusion | flops 2214592512 | bytes 11337728 | tf_op jit(solution)/shard_map/sjcd,jdgh->sjcgh/dot_general | solution.py:216
  286.2 4.6 %convert_bitcast_fusion = bf16[32,2,24,2048]{3,2,0,1:T(8,128)(2,1)} fusion(bf16[2,176,2048]{2,1,0:T(8,128)(2,1)S(1)} %copy-done.5, f32[32,2,24,2,176]{4,2,3,0,1:T(8,128)S(1)} %fusion.3), kind=kOutput, calls=%fused_computation.4 | convolution fusion | flops 1112064000 | bytes 9895936 | tf_op jit(solution)/shard_map/sjch,jhd->sjcd/dot_general | solution.py:223
  290.8 46.1 %reduce-scatter.2.cloned.1.call-done = bf16[32,2,24,256]{3,2,0,1:T(8,128)(2,1)} async-done(((bf16[32,2,24,2048]{3,2,0,1:T(8,128)(2,1)}), bf16[32,2,24,256]{3,2,0,1:T(8,128)(2,1)}) %reduce-scatter.2.cloned.1.call-update) | async-done | bytes 786448 | tf_op jit(solution)/shard_map/reduce_scatter | solution.py:226
  336.9 2.1 copy.80
  339.0 10.1 %all-to-all-start.6 = ((bf16[32,2,24,256]{3,2,1,0:T(8,128)(2,1)}), bf16[32,2,24,256]{3,2,1,0:T(8,128)(2,1)}, u32[]{:S(2)}, u32[]{:S(2)}) async-start(bf16[32,2,24,256]{3,2,1,0:T(8,128)(2,1)} %copy.80), calls=%async_computation.7 | async-start | bytes 1572864 | tf_op jit(solution)/shard_map/all_to_all | solution.py:229
  349.3 22.6 %all-to-all-done.6 = bf16[32,2,24,256]{3,2,1,0:T(8,128)(2,1)} async-done(((bf16[32,2,24,256]{3,2,1,0:T(8,128)(2,1)}), bf16[32,2,24,256]{3,2,1,0:T(8,128)(2,1)}, u32[]{:S(2)}, u32[]{:S(2)}) %all-to-all-start.6) | async-done | bytes 786464 | tf_op jit(solution)/shard_map/all_to_all | solution.py:229
  371.8 3.3 gather_fusion
  376.2 1.6 multiply_reduce_fusion.1
  377.9 1.5 add_convert_fusion
  (63 shorter events, 16.4 us)
Async XLA Ops:
  7.2 273.3 %copy-start = (bf16[2,2048,2,176]{1,3,2,0:T(8,128)(2,1)S(1)}, bf16[2,2048,2,176]{1,3,2,0:T(8,128)(2,1)}, u32[]{:S(2)}) copy-start(bf16[2,2048,2,176]{1,3,2,0:T(8,128)(2,1)} %param.26) | copy-start | bytes 8650756
  52.3 34.3 %all-to-all-start.2 = ((bf16[32,129,128]{2,1,0:T(8,128)(2,1)}), bf16[32,129,128]{2,1,0:T(8,128)(2,1)}, u32[]{:S(2)}, u32[]{:S(2)}) async-start(bf16[32,129,128]{2,1,0:T(8,128)(2,1)} %broadcast_in_dim.38), calls=%async_computation.2 | async-start | bytes 2228224 | tf_op jit(solution)/shard_map/all_to_all | solution.py:128
  86.6 35.6 %all-to-all-start.1 = ((bf16[32,1,144,128]{3,2,1,0:T(8,128)(2,1)}), bf16[32,1,144,128]{3,2,1,0:T(8,128)(2,1)}, u32[]{:S(2)}, u32[]{:S(2)}) async-start(bf16[32,1,144,128]{3,2,1,0:T(8,128)(2,1)} %shard_map.140), calls=%async_computation.1 | async-start | bytes 2359296 | tf_op jit(solution)/shard_map/all_to_all | solution.py:138
  122.1 36.1 %all-to-all-start.3 = ((bf16[32,1,144,128]{3,2,1,0:T(8,128)(2,1)}), bf16[32,1,144,128]{3,2,1,0:T(8,128)(2,1)}, u32[]{:S(2)}, u32[]{:S(2)}) async-start(bf16[32,1,144,128]{3,2,1,0:T(8,128)(2,1)} %shard_map.141), calls=%async_computation.3 | async-start | bytes 2359296 | tf_op jit(solution)/shard_map/all_to_all | solution.py:138
  127.5 3.2 copy-start.4
  127.5 3.3 copy-start.1
  166.3 4.5 %copy-start.2 = (s32[128,6]{0,1:T(8,128)S(1)}, s32[128,6]{0,1:T(8,128)}, u32[]{:S(2)}) copy-start(s32[128,6]{0,1:T(8,128)} %param.24) | copy-start | bytes 9220
  166.3 20.5 %all-to-all-start.4 = ((f32[128,8,256]{2,0,1:T(8,128)}), f32[128,8,256]{2,0,1:T(8,128)}, u32[]{:S(2)}, u32[]{:S(2)}) async-start(f32[128,8,256]{2,0,1:T(8,128)} %fusion.43), calls=%async_computation.4 | async-start | bytes 2097152 | tf_op jit(solution)/shard_map/all_to_all | solution.py:180
  170.7 109.8 %all-gather.2.cloned.1.call-start = ((), (), s32[]{:S(2)}) async-start(), calls=%async_computation.8 | async-start | bytes 7077888 | tf_op jit(solution)/shard_map/all_gather | solution.py:218
  239.7 97.3 %reduce-scatter.2.cloned.1.call-start = ((), (), s32[]{:S(2)}) async-start(), calls=%async_computation.9 | async-start | bytes 7077888 | tf_op jit(solution)/shard_map/reduce_scatter | solution.py:226
  280.5 5.7 %copy-start.5 = (bf16[2,176,2048]{2,1,0:T(8,128)(2,1)S(1)}, bf16[2,176,2048]{2,1,0:T(8,128)(2,1)}, u32[]{:S(2)}) copy-start(bf16[2,176,2048]{2,1,0:T(8,128)(2,1)} %param.27) | copy-start | bytes 4325380
  290.8 58.4 %copy-start.3 = (f32[128,6]{0,1:T(8,128)S(1)}, f32[128,6]{0,1:T(8,128)}, u32[]{:S(2)}) copy-start(f32[128,6]{0,1:T(8,128)} %param.25) | copy-start | bytes 9220
  339.0 32.8 %all-to-all-start.6 = ((bf16[32,2,24,256]{3,2,1,0:T(8,128)(2,1)}), bf16[32,2,24,256]{3,2,1,0:T(8,128)(2,1)}, u32[]{:S(2)}, u32[]{:S(2)}) async-start(bf16[32,2,24,256]{3,2,1,0:T(8,128)(2,1)} %copy.80), calls=%async_computation.7 | async-start | bytes 1572864 | tf_op jit(solution)/shard_map/all_to_all | solution.py:229
Sparse Core Ops, SparseCore 0:
  239.8 40.6 all-gather.1
  290.9 45.9 reduce-scatter.1
